TPU v7x, 32 devices: a whole 2x2x4 slice. The times are simulated.
32 devices in a mesh: groups: 2 (over x), chan: 16 (over z, y, core).
Axes of the slice: x: 2, y: 2, z: 4, core: 2. Of those that a mesh axis runs over, the one named last changes fastest.
Arguments:
- traces: float32 [2048, 1152], P(('groups', 'chan')), parts along dimension 0, as said below
- good_mask: int32 [2048], P(('groups', 'chan')), parts along dimension 0, may hold values 0 or 1
Outputs:
- correlations: bfloat16 [2048, 64, 1024], P(('groups', 'chan')), parts along dimension 0
There are 2 independent parts, one for each index of `groups`. A program takes and returns all parts, laid end to end along the dimension named above; each array names one. Nothing has to cross between parts.
Inputs may be any that keep to these rules, and one draw needn't show every extreme that they name: `traces`: traces of order one.
All inputs are finite; a program needn't handle non-finite values. No bound on the sum of `good_mask` on one device may be relied on, other than what follows from the above.
Results may differ from a plain program's by a relative error of at most 0.0053.
Values may be sent and summed in bfloat16 or wider, within the bound.
No kernel may reach another device: no remote copies, remote signals or barrier semaphores. Data moves between devices by JAX's collectives and lax.ppermute only.
A program may use at most 128 MiB of HBM per device.

v0:
```python
import math
import jax
import jax.numpy as jnp
from jax import lax
from jax.sharding import PartitionSpec as P

NW = 256
NF = 128
HOP = 128
LAGS = 64
NWIN = 8


def forward_table(width, bins):
    samples = jnp.arange(width)
    freqs = jnp.arange(1, bins + 1)
    phase = samples[:, None] * freqs[None, :] % width
    theta = 2.0 * math.pi * phase.astype(jnp.float32) / width
    hann = 0.5 - 0.5 * jnp.cos(2.0 * math.pi * samples.astype(jnp.float32) / width)
    return jnp.concatenate(
        [hann[:, None] * jnp.cos(theta), -hann[:, None] * jnp.sin(theta)], axis=1
    )


def lag_rotation(width, bins, lag_count):
    freqs = jnp.arange(1, bins + 1)
    lags = jnp.arange(lag_count) - lag_count // 2
    phase = freqs[:, None] * lags[None, :] % width
    theta = 2.0 * math.pi * phase.astype(jnp.float32) / width
    return (jnp.cos(theta), jnp.sin(theta))


def whiten(traces, good_mask):
    channels_here = traces.shape[0]
    good = good_mask.astype(jnp.float32)
    total, count = lax.psum((jnp.sum(traces * good[:, None], axis=0), jnp.sum(good)), "chan")
    common = total / jnp.maximum(count, 1.0)
    clean = (traces - common[None, :]) * good[:, None]
    halves = clean.reshape(channels_here, NWIN + 1, HOP)
    segments = jnp.concatenate([halves[:, :-1], halves[:, 1:]], axis=2)
    spectrum = jnp.einsum(
        "cwn,nk->wck", segments, forward_table(NW, NF), precision=lax.Precision.HIGHEST
    )
    real_part = spectrum[..., :NF]
    imag_part = spectrum[..., NF:]
    power = real_part * real_part + imag_part * imag_part
    magnitude = jnp.sqrt(power)
    level = jnp.sqrt(jnp.mean(power, axis=-1, keepdims=True) + 1e-06)
    denom = jnp.maximum(magnitude, 0.3 * level)
    return jnp.concatenate([real_part / denom, imag_part / denom], axis=-1).astype(jnp.bfloat16)


def shards(traces, good_mask):
    whitened = whiten(traces, good_mask)
    others = lax.all_gather(whitened, "chan", axis=1, tiled=True)
    own = whitened.astype(jnp.float32)
    own_real, own_imag = (own[..., :NF], own[..., NF:])
    cos, sin = lag_rotation(NW, NF, LAGS)
    scale = 1.0 / (NWIN * NF)
    cos = cos * scale
    sin = sin * scale
    rot_real = (
        own_real[:, :, None, :] * cos.T[None, None] - own_imag[:, :, None, :] * sin.T[None, None]
    )
    rot_imag = (
        own_real[:, :, None, :] * sin.T[None, None] + own_imag[:, :, None, :] * cos.T[None, None]
    )
    rotated = jnp.concatenate([rot_real, rot_imag], axis=-1).astype(jnp.bfloat16)
    result = jnp.einsum("wilk,wjk->ilj", rotated, others, preferred_element_type=jnp.float32)
    return result.astype(jnp.bfloat16)


def solution(mesh):
    placed = (P(("groups", "chan"), None), P(("groups", "chan")))
    return jax.shard_map(
        shards,
        mesh=mesh,
        in_specs=placed,
        out_specs=P(("groups", "chan"), None, None),
        check_vma=False,
    )
```

profile of v0, /device:TPU:0, one launch (start us, length us, event | category | flops | bytes accessed | tf_op | source)
XLA Modules:
  0.0 129.0 jit_solution(4269690971907902461)
XLA Ops:
  6.5 0.0 all-gather.2.cloned.1.call-start
  6.5 1.3 convert_reduce_fusion
  7.8 0.7 convert_element_type.48
  8.5 1.1 multiply_reduce_fusion
  9.6 36.6 %all-reduce = (f32[1152]{0:T(1024)S(1)}, f32[]{:T(128)}) all-reduce(f32[1152]{0:T(1024)S(1)} %multiply_reduce_fusion, f32[]{:T(128)} %convert_reduce_fusion), channel_id=1, replica_groups=mesh['groups'=2,'chan'=16] {'chan'}, use_global_device_ids=true, to_apply=%region_1.0 | all-reduce | flops 1153 | bytes 9224 | tf_op jit(solution)/shard_map/psum | solution.py:36
  46.9 1.1 subtract_multiply_fusion
  48.0 0.1 copy.10
  48.1 0.1 copy.11
  48.2 0.5 cosine_multiply_fusion
  48.7 0.6 convolution_bitcast_fusion
  49.3 0.1 fusion.25
  49.5 0.2 divide_convert_fusion.1
  49.6 0.8 pad_maximum_fusion
  50.4 0.0 all-gather.2.cloned.1.call-update
  50.5 0.2 copy.7
  50.6 0.2 copy.8
  50.8 0.2 cosine_multiply_fusion.1
  51.0 7.5 %subtract_convert_fusion = (bf16[8,64,64,128]{3,2,0,1:T(8,128)(2,1)}, bf16[8,64,64,128]{3,2,0,1:T(8,128)(2,1)}) fusion(f32[64,128]{1,0:T(8,128)S(1)} %get-tuple-element.18, f32[8,64,128]{2,0,1:T(8,128)S(1)} %copy.8, f32[64,128]{1,0:T(8,128)S(1)} %get-tuple-element.17, f32[8,64,128]{2,0,1:T(8,128)S(1)} %copy.7), kind=kLoop, calls=%fused_computation.6 | loop fusion | flops 33554432 | bytes 17367040 | tf_op jit(solution)/shard_map/convert
  58.5 39.7 %all-gather.2.cloned.1.call-done = bf16[8,1024,256]{2,1,0:T(8,128)(2,1)} async-done(((bf16[8,64,256]{2,1,0:T(8,128)(2,1)}), bf16[8,1024,256]{2,1,0:T(8,128)(2,1)}) %all-gather.2.cloned.1.call-update) | async-done | bytes 4194320 | tf_op jit(solution)/shard_map/all_gather | solution.py:55
  98.2 24.0 %bitcast_convert_fusion = bf16[64,64,1024]{2,1,0:T(8,128)(2,1)} fusion(bf16[8,64,64,128]{3,2,0,1:T(8,128)(2,1)} %get-tuple-element.8, bf16[8,64,64,128]{3,2,0,1:T(8,128)(2,1)} %get-tuple-element.7, bf16[8,1024,256]{2,1,0:T(8,128)(2,1)} %all-gather.2.cloned.1.call-done), kind=kOutput, calls=%fused_computation.4 | convolution fusion | flops 17217617920 | bytes 29360128 | tf_op jit(solution)/shard_map/wilk,wjk->ilj/dot_general | solution.py:69
  (8 shorter events, 0.2 us)
Async XLA Ops:
  6.5 91.7 %all-gather.2.cloned.1.call-start = ((), (), s32[]{:S(2)}) async-start(), calls=%async_computation | async-start | bytes 4456448 | tf_op jit(solution)/shard_map/all_gather | solution.py:55
Sparse Core Ops, SparseCore 0:
  50.5 47.6 all-gather.1
where the time goes:
time: 129 us
  waiting for transfers between devices  39.7 us (31%)
  blocking collectives  36.6 us (28%)
  matrix products  24.6 us (19%)
  between operations  14.1 us (11%)
  other arithmetic  13.4 us (10%)
    all_gather x1, waiting for transfers between devices, shards(): others = lax.all_gather(whitened, 'chan', axis=1, tiled=True)  39.7 us
    psum x1, blocking collectives, whiten(): lax.psum((jnp.sum(traces * good[:, None], axis=0), jnp.sum(good)), 'chan')  36.6 us
    dot_general x1, matrix products, shards(): jnp.einsum('wilk,wjk->ilj', rotated, others, preferred_element_type=jnp.f...  24 us
    another operation x2, other arithmetic  7.65 us
  transfers between devices with their start and end apart: 1, of which 1 were waited for; matrix products, arithmetic and copies ran while one was open for 6% of the time, Pallas kernels for 0%

commit v1 on v0

--- a/solution.py
+++ b/solution.py
@@ -9,6 +9,30 @@
 HOP = 128
 LAGS = 64
 NWIN = 8
+
+
+def set_block(panel, array_dim, mat, d0):
+    val = jax.lax.psum(1, "chan")
+    then = jax.lax.axis_index("chan")
+    right_arr, long_array, reached = (val, then, panel.shape[array_dim])
+    y1, state_now = ([], [])
+    carry = w1 = panel
+    for kk in range(right_arr // 2 + 1):
+        part_next = mat(carry, (long_array - kk) % right_arr * reached)
+        y1.append(part_next)
+        if 0 < kk < right_arr - right_arr // 2:
+            current_block = mat(w1, (long_array + kk) % right_arr * reached)
+            state_now.append(current_block)
+        carry = jax.lax.ppermute(
+            carry, "chan", [(i, (i + 1) % right_arr) for i in range(right_arr)]
+        )
+        w1 = jax.lax.ppermute(w1, "chan", [(i, (i - 1) % right_arr) for i in range(right_arr)])
+    ready = jnp.roll(
+        jnp.concatenate([*y1[::-1], *state_now], axis=d0),
+        (long_array - right_arr // 2) * y1[0].shape[d0],
+        d0,
+    )
+    return ready
 
 
 def forward_table(width, bins):
@@ -52,7 +76,6 @@
 
 def shards(traces, good_mask):
     whitened = whiten(traces, good_mask)
-    others = lax.all_gather(whitened, "chan", axis=1, tiled=True)
     own = whitened.astype(jnp.float32)
     own_real, own_imag = (own[..., :NF], own[..., NF:])
     cos, sin = lag_rotation(NW, NF, LAGS)
@@ -66,7 +89,14 @@
         own_real[:, :, None, :] * sin.T[None, None] + own_imag[:, :, None, :] * cos.T[None, None]
     )
     rotated = jnp.concatenate([rot_real, rot_imag], axis=-1).astype(jnp.bfloat16)
-    result = jnp.einsum("wilk,wjk->ilj", rotated, others, preferred_element_type=jnp.float32)
+    result = set_block(
+        whitened,
+        1,
+        lambda shard, start: jnp.einsum(
+            "wilk,wjk->ilj", rotated, shard, preferred_element_type=jnp.float32
+        ),
+        2,
+    )
     return result.astype(jnp.bfloat16)
 
 

time: 129 us -> 235 us (1.82); the launches traced: 129 us -> 231 us
  matrix products: 24.6 us -> 99.2 us
  local copies, waits for them, and re-layouts: 0.55 us -> 52.1 us
  waiting for transfers between devices: 39.7 us -> 5.6 us
  starting transfers between devices: 0.01 us -> 26.8 us
  between operations: 14.1 us -> 0.87 us
  other arithmetic: 13.4 us -> 9.64 us
    dot_general x1 -> x16, matrix products: 24 us -> 98.6 us  [shards(): jnp.einsum('wilk,wjk->ilj', rotated, shard, preferred_element_type=jnp.fl...]
    all_gather x1 -> x0, waiting for transfers between devices: 39.7 us -> none  [shards(): others = lax.all_gather(whitened, 'chan', axis=1, tiled=True)]
    concatenate x0 -> x1, local copies, waits for them, and re-layouts: none -> 39 us  [set_block(): jnp.roll(jnp.concatenate([*y1[::-1], *state_now], axis=d0), (long_array -...]
    ppermute x0 -> x15, starting transfers between devices: none -> 26.8 us  [the longest x7 26.3 us: set_block(): jax.lax.ppermute(w1, 'chan', [(i, (i - 1) % right_arr) for i in range(rig...]
    convert_element_type x0 -> x1, local copies, waits for them, and re-layouts: none -> 12.6 us  [shards(): return result.astype(jnp.bfloat16)]
    ppermute x0 -> x15, waiting for transfers between devices: none -> 5.6 us  [the longest x8 5.58 us: set_block(): jax.lax.ppermute(carry, 'chan', [(i, (i + 1) % right_arr) for i in range(...]
    another operation x2, other arithmetic: 7.65 us -> 4.59 us
  transfers between devices with their start and end apart: 1 -> 15, of which waited for: 1 -> 2; matrix products, arithmetic and copies ran while one was open for 6% -> 42% of each run, Pallas kernels for 0% -> 0%
where the time goes in v1:
time: 235 us; the launch traced here: 231 us
  matrix products  99.2 us (42%)
  local copies, waits for them, and re-layouts  52.1 us (22%)
  blocking collectives  36.6 us (16%)
  starting transfers between devices  26.8 us (11%)
  other arithmetic  9.64 us (4%)
  waiting for transfers between devices  5.6 us (2%)
    dot_general x16, matrix products, shards(): jnp.einsum('wilk,wjk->ilj', rotated, shard, preferred_element_type=jnp.fl...  98.6 us
    concatenate x1, local copies, waits for them, and re-layouts, set_block(): jnp.roll(jnp.concatenate([*y1[::-1], *state_now], axis=d0), (long_array -...  39 us
    psum x1, blocking collectives, whiten(): lax.psum((jnp.sum(traces * good[:, None], axis=0), jnp.sum(good)), 'chan')  36.6 us
    ppermute x7, starting transfers between devices, set_block(): jax.lax.ppermute(w1, 'chan', [(i, (i - 1) % right_arr) for i in range(rig...  26.3 us
    convert_element_type x1, local copies, waits for them, and re-layouts, shards(): return result.astype(jnp.bfloat16)  12.6 us
    ppermute x8, waiting for transfers between devices, set_block(): jax.lax.ppermute(carry, 'chan', [(i, (i + 1) % right_arr) for i in range(...  5.58 us
  transfers between devices with their start and end apart: 15, of which 2 were waited for; matrix products, arithmetic and copies ran while one was open for 42% of the time, Pallas kernels for 0%

profile of v1, /device:TPU:0, one launch (start us, length us, event | category | flops | bytes accessed | tf_op | source)
XLA Modules:
  0.0 230.9 jit_solution(13232363081643385098)
XLA Ops:
  0.0 0.7 convert_element_type.48
  0.7 1.3 convert_reduce_fusion
  2.0 1.1 multiply_reduce_fusion
  3.0 36.6 %all-reduce = (f32[1152]{0:T(1024)S(1)}, f32[]{:T(128)}) all-reduce(f32[1152]{0:T(1024)S(1)} %multiply_reduce_fusion, f32[]{:T(128)} %convert_reduce_fusion), channel_id=1, replica_groups=mesh['groups'=2,'chan'=16] {'chan'}, use_global_device_ids=true, to_apply=%region_1.0 | all-reduce | flops 1153 | bytes 9224 | tf_op jit(solution)/shard_map/psum | solution.py:60
  40.3 1.1 subtract_multiply_fusion
  41.5 0.1 copy.25
  41.6 0.1 copy.26
  41.6 0.5 cosine_multiply_fusion
  42.2 0.6 convolution_bitcast_fusion.16
  42.8 0.1 fusion.32
  42.9 0.2 divide_convert_fusion.1
  43.1 0.1 fusion.33
  43.2 0.1 collective-permute-start.8
  43.2 0.5 collective-permute-start
  43.8 0.2 copy.7
  44.0 0.2 copy.8
  44.1 0.2 cosine_multiply_fusion.1
  44.3 4.4 %subtract_convert_fusion = (bf16[8,64,64,128]{3,2,0,1:T(8,128)(2,1)S(1)}, bf16[8,64,64,128]{3,2,0,1:T(8,128)(2,1)S(1)}) fusion(f32[64,128]{1,0:T(8,128)S(1)} %get-tuple-element.18, f32[8,64,128]{2,0,1:T(8,128)S(1)} %copy.8, f32[64,128]{1,0:T(8,128)S(1)} %get-tuple-element.17, f32[8,64,128]{2,0,1:T(8,128)S(1)} %copy.7), kind=kLoop, calls=%fused_computation.3 | loop fusion | flops 33554432 | bytes 17367040 | tf_op jit(solution)/shard_map/convert
  48.8 0.0 copy-start.1
  48.8 6.3 %convolution_bitcast_fusion.7 = bf16[64,64,64]{2,1,0:T(8,128)(2,1)} fusion(bf16[8,64,128]{2,1,0:T(8,128)(2,1)S(1)} %get-tuple-element.10, bf16[8,64,128]{2,1,0:T(8,128)(2,1)S(1)} %get-tuple-element.9, bf16[8,64,64,128]{3,2,0,1:T(8,128)(2,1)S(1)} %get-tuple-element.8, bf16[8,64,64,128]{3,2,0,1:T(8,128)(2,1)S(1)} %get-tuple-element.7), kind=kOutput, calls=%fused_computation.11 | convolution fusion | flops 1107820544 | bytes 17563648 | tf_op jit(solution)/shard_map/wilk,wjk->ilj/dot_general | solution.py:95
  55.1 0.0 copy-done.1
  55.1 0.0 collective-permute-done.8
  55.1 4.0 %collective-permute-start.9 = (bf16[8,64,256]{2,1,0:T(8,128)(2,1)S(1)}, bf16[8,64,256]{2,1,0:T(8,128)(2,1)S(1)}, u32[]{:S(2)}, u32[]{:S(2)}) collective-permute-start(bf16[8,64,256]{2,1,0:T(8,128)(2,1)S(1)} %collective-permute-done.8), channel_id=1, source_target_pairs={{0,15},{1,0},{2,1},{3,2},{4,3},{5,4},{6,5},{7,6},{8,7},{9,8},{10,9... | collective-permute-start | bytes 786440 | tf_op jit(solution)/shard_map/ppermute | solution.py:29
  59.1 9.2 %convolution_bitcast_fusion.6 = bf16[64,64,64]{2,1,0:T(8,128)(2,1)} fusion(bf16[8,64,256]{2,1,0:T(8,128)(2,1)S(1)} %collective-permute-done.8, bf16[8,64,64,128]{3,2,0,1:T(8,128)(2,1)} %copy-done.1, bf16[8,64,64,128]{3,2,0,1:T(8,128)(2,1)} %copy-done), kind=kOutput, calls=%fused_computation.10 | convolution fusion | flops 1107296256 | bytes 17563648 | tf_op jit(solution)/shard_map/wilk,wjk->ilj/dot_general | solution.py:95
  68.4 0.0 collective-permute-done
  68.4 9.2 %convolution_bitcast_fusion.8 = bf16[64,64,64]{2,1,0:T(8,128)(2,1)} fusion(bf16[8,64,256]{2,1,0:T(8,128)(2,1)S(1)} %collective-permute-done, bf16[8,64,64,128]{3,2,0,1:T(8,128)(2,1)} %copy-done.1, bf16[8,64,64,128]{3,2,0,1:T(8,128)(2,1)} %copy-done), kind=kOutput, calls=%fused_computation.12 | convolution fusion | flops 1107296256 | bytes 17563648 | tf_op jit(solution)/shard_map/wilk,wjk->ilj/dot_general | solution.py:95
  77.6 0.0 collective-permute-start.1
  77.6 0.0 collective-permute-done.9
  77.6 4.4 %collective-permute-start.10 = (bf16[8,64,256]{2,1,0:T(8,128)(2,1)S(1)}, bf16[8,64,256]{2,1,0:T(8,128)(2,1)S(1)}, u32[]{:S(2)}, u32[]{:S(2)}) collective-permute-start(bf16[8,64,256]{2,1,0:T(8,128)(2,1)S(1)} %collective-permute-done.9), channel_id=1, source_target_pairs={{0,15},{1,0},{2,1},{3,2},{4,3},{5,4},{6,5},{7,6},{8,7},{9,8},{10,9... | collective-permute-start | bytes 786440 | tf_op jit(solution)/shard_map/ppermute | solution.py:29
  82.1 5.7 %convolution_bitcast_fusion.5 = bf16[64,64,64]{2,1,0:T(8,128)(2,1)} fusion(bf16[8,64,256]{2,1,0:T(8,128)(2,1)S(1)} %collective-permute-done.9, bf16[8,64,64,128]{3,2,0,1:T(8,128)(2,1)S(1)} %bitcast.104, bf16[8,64,64,128]{3,2,0,1:T(8,128)(2,1)S(1)} %bitcast.102), kind=kOutput, calls=%fused_computation.9 | convolution fusion | flops 1107296256 | bytes 17563648 | tf_op jit(solution)/shard_map/wilk,wjk->ilj/dot_general | solution.py:95
  87.8 0.0 collective-permute-done.1
  87.8 5.7 %convolution_bitcast_fusion.9 = bf16[64,64,64]{2,1,0:T(8,128)(2,1)} fusion(bf16[8,64,256]{2,1,0:T(8,128)(2,1)S(1)} %collective-permute-done.1, bf16[8,64,64,128]{3,2,0,1:T(8,128)(2,1)S(1)} %bitcast.104, bf16[8,64,64,128]{3,2,0,1:T(8,128)(2,1)S(1)} %bitcast.102), kind=kOutput, calls=%fused_computation.13 | convolution fusion | flops 1107296256 | bytes 17563648 | tf_op jit(solution)/shard_map/wilk,wjk->ilj/dot_general | solution.py:95
  93.5 0.0 collective-permute-start.2
  93.5 4.4 %collective-permute-start.11 = (bf16[8,64,256]{2,1,0:T(8,128)(2,1)S(1)}, bf16[8,64,256]{2,1,0:T(8,128)(2,1)S(1)}, u32[]{:S(2)}, u32[]{:S(2)}) collective-permute-start(bf16[8,64,256]{2,1,0:T(8,128)(2,1)S(1)} %collective-permute-done.10), channel_id=1, source_target_pairs={{0,15},{1,0},{2,1},{3,2},{4,3},{5,4},{6,5},{7,6},{8,7},{9,8},{10,9... | collective-permute-start | bytes 786440 | tf_op jit(solution)/shard_map/ppermute | solution.py:29
  97.9 5.7 %convolution_bitcast_fusion.4 = bf16[64,64,64]{2,1,0:T(8,128)(2,1)} fusion(bf16[8,64,256]{2,1,0:T(8,128)(2,1)S(1)} %collective-permute-done.10, bf16[8,64,64,128]{3,2,0,1:T(8,128)(2,1)S(1)} %bitcast.104, bf16[8,64,64,128]{3,2,0,1:T(8,128)(2,1)S(1)} %bitcast.102), kind=kOutput, calls=%fused_computation.8 | convolution fusion | flops 1107296256 | bytes 17563648 | tf_op jit(solution)/shard_map/wilk,wjk->ilj/dot_general | solution.py:95
  103.6 0.0 collective-permute-done.2
  103.6 5.7 %convolution_bitcast_fusion.10 = bf16[64,64,64]{2,1,0:T(8,128)(2,1)} fusion(bf16[8,64,256]{2,1,0:T(8,128)(2,1)S(1)} %collective-permute-done.2, bf16[8,64,64,128]{3,2,0,1:T(8,128)(2,1)S(1)} %bitcast.104, bf16[8,64,64,128]{3,2,0,1:T(8,128)(2,1)S(1)} %bitcast.102), kind=kOutput, calls=%fused_computation.14 | convolution fusion | flops 1107296256 | bytes 17563648 | tf_op jit(solution)/shard_map/wilk,wjk->ilj/dot_general | solution.py:95
  109.3 0.0 collective-permute-start.3
  109.3 0.0 collective-permute-done.11
  109.3 4.4 %collective-permute-start.12 = (bf16[8,64,256]{2,1,0:T(8,128)(2,1)S(1)}, bf16[8,64,256]{2,1,0:T(8,128)(2,1)S(1)}, u32[]{:S(2)}, u32[]{:S(2)}) collective-permute-start(bf16[8,64,256]{2,1,0:T(8,128)(2,1)S(1)} %collective-permute-done.11), channel_id=1, source_target_pairs={{0,15},{1,0},{2,1},{3,2},{4,3},{5,4},{6,5},{7,6},{8,7},{9,8},{10,9... | collective-permute-start | bytes 786440 | tf_op jit(solution)/shard_map/ppermute | solution.py:29
  113.7 5.7 %convolution_bitcast_fusion.3 = bf16[64,64,64]{2,1,0:T(8,128)(2,1)} fusion(bf16[8,64,256]{2,1,0:T(8,128)(2,1)S(1)} %collective-permute-done.11, bf16[8,64,64,128]{3,2,0,1:T(8,128)(2,1)S(1)} %bitcast.104, bf16[8,64,64,128]{3,2,0,1:T(8,128)(2,1)S(1)} %bitcast.102), kind=kOutput, calls=%fused_computation.7 | convolution fusion | flops 1107296256 | bytes 17563648 | tf_op jit(solution)/shard_map/wilk,wjk->ilj/dot_general | solution.py:95
  119.4 0.0 collective-permute-done.3
  119.4 5.7 %convolution_bitcast_fusion.11 = bf16[64,64,64]{2,1,0:T(8,128)(2,1)} fusion(bf16[8,64,256]{2,1,0:T(8,128)(2,1)S(1)} %collective-permute-done.3, bf16[8,64,64,128]{3,2,0,1:T(8,128)(2,1)S(1)} %bitcast.104, bf16[8,64,64,128]{3,2,0,1:T(8,128)(2,1)S(1)} %bitcast.102), kind=kOutput, calls=%fused_computation.15 | convolution fusion | flops 1107296256 | bytes 17563648 | tf_op jit(solution)/shard_map/wilk,wjk->ilj/dot_general | solution.py:95
  125.1 0.0 collective-permute-start.4
  125.1 0.0 collective-permute-done.12
  125.1 4.4 %collective-permute-start.13 = (bf16[8,64,256]{2,1,0:T(8,128)(2,1)S(1)}, bf16[8,64,256]{2,1,0:T(8,128)(2,1)S(1)}, u32[]{:S(2)}, u32[]{:S(2)}) collective-permute-start(bf16[8,64,256]{2,1,0:T(8,128)(2,1)S(1)} %collective-permute-done.12), channel_id=1, source_target_pairs={{0,15},{1,0},{2,1},{3,2},{4,3},{5,4},{6,5},{7,6},{8,7},{9,8},{10,9... | collective-permute-start | bytes 786440 | tf_op jit(solution)/shard_map/ppermute | solution.py:29
  129.6 5.7 %convolution_bitcast_fusion.2 = bf16[64,64,64]{2,1,0:T(8,128)(2,1)} fusion(bf16[8,64,256]{2,1,0:T(8,128)(2,1)S(1)} %collective-permute-done.12, bf16[8,64,64,128]{3,2,0,1:T(8,128)(2,1)S(1)} %bitcast.104, bf16[8,64,64,128]{3,2,0,1:T(8,128)(2,1)S(1)} %bitcast.102), kind=kOutput, calls=%fused_computation.6 | convolution fusion | flops 1107296256 | bytes 17563648 | tf_op jit(solution)/shard_map/wilk,wjk->ilj/dot_general | solution.py:95
  135.2 0.0 collective-permute-done.4
  135.2 5.7 %convolution_bitcast_fusion.12 = bf16[64,64,64]{2,1,0:T(8,128)(2,1)} fusion(bf16[8,64,256]{2,1,0:T(8,128)(2,1)S(1)} %collective-permute-done.4, bf16[8,64,64,128]{3,2,0,1:T(8,128)(2,1)S(1)} %bitcast.104, bf16[8,64,64,128]{3,2,0,1:T(8,128)(2,1)S(1)} %bitcast.102), kind=kOutput, calls=%fused_computation.16 | convolution fusion | flops 1107296256 | bytes 17563648 | tf_op jit(solution)/shard_map/wilk,wjk->ilj/dot_general | solution.py:95
  140.9 0.0 collective-permute-start.5
  140.9 0.0 collective-permute-done.13
  140.9 4.4 %collective-permute-start.14 = (bf16[8,64,256]{2,1,0:T(8,128)(2,1)S(1)}, bf16[8,64,256]{2,1,0:T(8,128)(2,1)S(1)}, u32[]{:S(2)}, u32[]{:S(2)}) collective-permute-start(bf16[8,64,256]{2,1,0:T(8,128)(2,1)S(1)} %collective-permute-done.13), channel_id=1, source_target_pairs={{0,15},{1,0},{2,1},{3,2},{4,3},{5,4},{6,5},{7,6},{8,7},{9,8},{10,9... | collective-permute-start | bytes 786440 | tf_op jit(solution)/shard_map/ppermute | solution.py:29
  145.4 5.7 %convolution_bitcast_fusion.1 = bf16[64,64,64]{2,1,0:T(8,128)(2,1)} fusion(bf16[8,64,256]{2,1,0:T(8,128)(2,1)S(1)} %collective-permute-done.13, bf16[8,64,64,128]{3,2,0,1:T(8,128)(2,1)S(1)} %bitcast.104, bf16[8,64,64,128]{3,2,0,1:T(8,128)(2,1)S(1)} %bitcast.102), kind=kOutput, calls=%fused_computation.5 | convolution fusion | flops 1107296256 | bytes 17563648 | tf_op jit(solution)/shard_map/wilk,wjk->ilj/dot_general | solution.py:95
  151.0 0.0 collective-permute-done.5
  151.0 0.0 collective-permute-start.6
  151.0 5.7 %convolution_bitcast_fusion.13 = bf16[64,64,64]{2,1,0:T(8,128)(2,1)} fusion(bf16[8,64,256]{2,1,0:T(8,128)(2,1)S(1)} %collective-permute-done.5, bf16[8,64,64,128]{3,2,0,1:T(8,128)(2,1)S(1)} %bitcast.104, bf16[8,64,64,128]{3,2,0,1:T(8,128)(2,1)S(1)} %bitcast.102), kind=kOutput, calls=%fused_computation.17 | convolution fusion | flops 1107296256 | bytes 17563648 | tf_op jit(solution)/shard_map/wilk,wjk->ilj/dot_general | solution.py:95
  156.8 2.8 %collective-permute-done.6 = bf16[8,64,256]{2,1,0:T(8,128)(2,1)S(1)} collective-permute-done((bf16[8,64,256]{2,1,0:T(8,128)(2,1)S(1)}, bf16[8,64,256]{2,1,0:T(8,128)(2,1)S(1)}, u32[]{:S(2)}, u32[]{:S(2)}) %collective-permute-start.6) | collective-permute-done | bytes 262176 | tf_op jit(solution)/shard_map/ppermute | solution.py:26
  159.5 5.7 %convolution_bitcast_fusion.14 = bf16[64,64,64]{2,1,0:T(8,128)(2,1)} fusion(bf16[8,64,256]{2,1,0:T(8,128)(2,1)S(1)} %collective-permute-done.6, bf16[8,64,64,128]{3,2,0,1:T(8,128)(2,1)S(1)} %bitcast.104, bf16[8,64,64,128]{3,2,0,1:T(8,128)(2,1)S(1)} %bitcast.102), kind=kOutput, calls=%fused_computation.18 | convolution fusion | flops 1107296256 | bytes 17563648 | tf_op jit(solution)/shard_map/wilk,wjk->ilj/dot_general | solution.py:95
  165.2 0.0 collective-permute-start.7
  165.2 5.7 %convolution_bitcast_fusion = bf16[64,64,64]{2,1,0:T(8,128)(2,1)} fusion(bf16[8,64,256]{2,1,0:T(8,128)(2,1)S(1)} %collective-permute-done.14, bf16[8,64,64,128]{3,2,0,1:T(8,128)(2,1)S(1)} %bitcast.104, bf16[8,64,64,128]{3,2,0,1:T(8,128)(2,1)S(1)} %bitcast.102), kind=kOutput, calls=%fused_computation.4 | convolution fusion | flops 1107296256 | bytes 17563648 | tf_op jit(solution)/shard_map/wilk,wjk->ilj/dot_general | solution.py:95
  170.9 2.8 %collective-permute-done.7 = bf16[8,64,256]{2,1,0:T(8,128)(2,1)S(1)} collective-permute-done((bf16[8,64,256]{2,1,0:T(8,128)(2,1)S(1)}, bf16[8,64,256]{2,1,0:T(8,128)(2,1)S(1)}, u32[]{:S(2)}, u32[]{:S(2)}) %collective-permute-start.7) | collective-permute-done | bytes 262176 | tf_op jit(solution)/shard_map/ppermute | solution.py:26
  173.7 5.7 %convolution_bitcast_fusion.15 = bf16[64,64,64]{2,1,0:T(8,128)(2,1)} fusion(bf16[8,64,256]{2,1,0:T(8,128)(2,1)S(1)} %collective-permute-done.7, bf16[8,64,64,128]{3,2,0,1:T(8,128)(2,1)S(1)} %bitcast.104, bf16[8,64,64,128]{3,2,0,1:T(8,128)(2,1)S(1)} %bitcast.102), kind=kOutput, calls=%fused_computation.19 | convolution fusion | flops 1107296256 | bytes 17563648 | tf_op jit(solution)/shard_map/wilk,wjk->ilj/dot_general | solution.py:95
  179.4 39.0 %concatenate.24 = bf16[64,64,2048]{2,1,0:T(8,128)(2,1)} concatenate(bf16[64,64,64]{2,1,0:T(8,128)(2,1)} %convolution_bitcast_fusion.15, bf16[64,64,64]{2,1,0:T(8,128)(2,1)} %convolution_bitcast_fusion.14, bf16[64,64,64]{2,1,0:T(8,128)(2,1)} %convolution_bitcast_fusion.13, bf16[64,64,64]{2,1,0:T(8,128)(2,1)} %convolution_bitcast_fusion.12, ...), dimensions={2} | concatenate | bytes 33554432 | tf_op jit(solution)/shard_map/jit(_roll_dynamic)/concatenate | solution.py:30
  218.3 12.6 %dynamic-slice_convert_fusion = bf16[64,64,1024]{2,1,0:T(8,128)(2,1)} fusion(bf16[64,64,2048]{2,1,0:T(8,128)(2,1)} %concatenate.24, s32[]{:T(128)S(6)} %select_n.45), kind=kLoop, calls=%fused_computation.1 | loop fusion | bytes 16777220 | tf_op jit(solution)/shard_map/convert_element_type | solution.py:100
  (28 shorter events, 0.2 us)
Async XLA Ops:
  43.2 11.9 %collective-permute-start.8 = (bf16[8,64,256]{2,1,0:T(8,128)(2,1)S(1)}, bf16[8,64,256]{2,1,0:T(8,128)(2,1)S(1)}, u32[]{:S(2)}, u32[]{:S(2)}) collective-permute-start(bf16[8,64,256]{2,1,0:T(8,128)(2,1)S(1)} %get-tuple-element.16), channel_id=1, source_target_pairs={{0,15},{1,0},{2,1},{3,2},{4,3},{5,4},{6,5},{7,6},{8,7},{9,8},{10,9... | collective-permute-start | bytes 786440 | tf_op jit(solution)/shard_map/ppermute | solution.py:29
  43.2 25.1 %collective-permute-start = (bf16[8,64,256]{2,1,0:T(8,128)(2,1)S(1)}, bf16[8,64,256]{2,1,0:T(8,128)(2,1)S(1)}, u32[]{:S(2)}, u32[]{:S(2)}) collective-permute-start(bf16[8,64,256]{2,1,0:T(8,128)(2,1)S(1)} %get-tuple-element.16), channel_id=1, source_target_pairs={{0,1},{1,2},{2,3},{3,4},{4,5},{5,6},{6,7},{7,8},{8,9},{9,10},{10,1... | collective-permute-start | bytes 786440 | tf_op jit(solution)/shard_map/ppermute | solution.py:26
  48.8 6.3 %copy-start = (bf16[8,64,64,128]{3,2,0,1:T(8,128)(2,1)}, bf16[8,64,64,128]{3,2,0,1:T(8,128)(2,1)S(1)}, u32[]{:S(2)}) copy-start(bf16[8,64,64,128]{3,2,0,1:T(8,128)(2,1)S(1)} %get-tuple-element.7) | copy-start | bytes 25165828
  48.8 6.3 %copy-start.1 = (bf16[8,64,64,128]{3,2,0,1:T(8,128)(2,1)}, bf16[8,64,64,128]{3,2,0,1:T(8,128)(2,1)S(1)}, u32[]{:S(2)}) copy-start(bf16[8,64,64,128]{3,2,0,1:T(8,128)(2,1)S(1)} %get-tuple-element.8) | copy-start | bytes 25165828
  55.1 22.5 %collective-permute-start.9 = (bf16[8,64,256]{2,1,0:T(8,128)(2,1)S(1)}, bf16[8,64,256]{2,1,0:T(8,128)(2,1)S(1)}, u32[]{:S(2)}, u32[]{:S(2)}) collective-permute-start(bf16[8,64,256]{2,1,0:T(8,128)(2,1)S(1)} %collective-permute-done.8), channel_id=1, source_target_pairs={{0,15},{1,0},{2,1},{3,2},{4,3},{5,4},{6,5},{7,6},{8,7},{9,8},{10,9... | collective-permute-start | bytes 786440 | tf_op jit(solution)/shard_map/ppermute | solution.py:29
  59.1 22.9 %slice-start = ((s8[8388608]{0:T(1024)(128)(4,1)}), s8[4194304]{0:T(1024)(128)(4,1)S(1)}, s32[]{:S(2)}) async-start(s8[8388608]{0:T(1024)(128)(4,1)} %bitcast.101), calls=%async_computation | async-start | bytes 8388608
  59.1 22.9 %slice-start.2 = ((s8[8388608]{0:T(1024)(128)(4,1)}), s8[4194304]{0:T(1024)(128)(4,1)S(1)}, s32[]{:S(2)}) async-start(s8[8388608]{0:T(1024)(128)(4,1)} %bitcast.103), calls=%async_computation.2 | async-start | bytes 8388608
  68.3 13.7 %slice-start.1 = ((s8[8388608]{0:T(1024)(128)(4,1)}), s8[4194304]{0:T(1024)(128)(4,1)S(1)}, s32[]{:S(2)}) async-start(s8[8388608]{0:T(1024)(128)(4,1)} %bitcast.101), calls=%async_computation.1 | async-start | bytes 8388608
  68.4 13.7 %slice-start.3 = ((s8[8388608]{0:T(1024)(128)(4,1)}), s8[4194304]{0:T(1024)(128)(4,1)S(1)}, s32[]{:S(2)}) async-start(s8[8388608]{0:T(1024)(128)(4,1)} %bitcast.103), calls=%async_computation.3 | async-start | bytes 8388608
  77.6 10.2 %collective-permute-start.1 = (bf16[8,64,256]{2,1,0:T(8,128)(2,1)S(1)}, bf16[8,64,256]{2,1,0:T(8,128)(2,1)S(1)}, u32[]{:S(2)}, u32[]{:S(2)}) collective-permute-start(bf16[8,64,256]{2,1,0:T(8,128)(2,1)S(1)} %collective-permute-done), channel_id=1, source_target_pairs={{0,1},{1,2},{2,3},{3,4},{4,5},{5,6},{6,7},{7,8},{8,9},{9,10},{10,1... | collective-permute-start | bytes 786440 | tf_op jit(solution)/shard_map/ppermute | solution.py:26
  77.6 15.9 %collective-permute-start.10 = (bf16[8,64,256]{2,1,0:T(8,128)(2,1)S(1)}, bf16[8,64,256]{2,1,0:T(8,128)(2,1)S(1)}, u32[]{:S(2)}, u32[]{:S(2)}) collective-permute-start(bf16[8,64,256]{2,1,0:T(8,128)(2,1)S(1)} %collective-permute-done.9), channel_id=1, source_target_pairs={{0,15},{1,0},{2,1},{3,2},{4,3},{5,4},{6,5},{7,6},{8,7},{9,8},{10,9... | collective-permute-start | bytes 786440 | tf_op jit(solution)/shard_map/ppermute | solution.py:29
  93.5 10.2 %collective-permute-start.2 = (bf16[8,64,256]{2,1,0:T(8,128)(2,1)S(1)}, bf16[8,64,256]{2,1,0:T(8,128)(2,1)S(1)}, u32[]{:S(2)}, u32[]{:S(2)}) collective-permute-start(bf16[8,64,256]{2,1,0:T(8,128)(2,1)S(1)} %collective-permute-done.1), channel_id=1, source_target_pairs={{0,1},{1,2},{2,3},{3,4},{4,5},{5,6},{6,7},{7,8},{8,9},{9,10},{10,1... | collective-permute-start | bytes 786440 | tf_op jit(solution)/shard_map/ppermute | solution.py:26
  93.5 15.8 %collective-permute-start.11 = (bf16[8,64,256]{2,1,0:T(8,128)(2,1)S(1)}, bf16[8,64,256]{2,1,0:T(8,128)(2,1)S(1)}, u32[]{:S(2)}, u32[]{:S(2)}) collective-permute-start(bf16[8,64,256]{2,1,0:T(8,128)(2,1)S(1)} %collective-permute-done.10), channel_id=1, source_target_pairs={{0,15},{1,0},{2,1},{3,2},{4,3},{5,4},{6,5},{7,6},{8,7},{9,8},{10,9... | collective-permute-start | bytes 786440 | tf_op jit(solution)/shard_map/ppermute | solution.py:29
  109.3 10.1 %collective-permute-start.3 = (bf16[8,64,256]{2,1,0:T(8,128)(2,1)S(1)}, bf16[8,64,256]{2,1,0:T(8,128)(2,1)S(1)}, u32[]{:S(2)}, u32[]{:S(2)}) collective-permute-start(bf16[8,64,256]{2,1,0:T(8,128)(2,1)S(1)} %collective-permute-done.2), channel_id=1, source_target_pairs={{0,1},{1,2},{2,3},{3,4},{4,5},{5,6},{6,7},{7,8},{8,9},{9,10},{10,1... | collective-permute-start | bytes 786440 | tf_op jit(solution)/shard_map/ppermute | solution.py:26
  109.3 15.8 %collective-permute-start.12 = (bf16[8,64,256]{2,1,0:T(8,128)(2,1)S(1)}, bf16[8,64,256]{2,1,0:T(8,128)(2,1)S(1)}, u32[]{:S(2)}, u32[]{:S(2)}) collective-permute-start(bf16[8,64,256]{2,1,0:T(8,128)(2,1)S(1)} %collective-permute-done.11), channel_id=1, source_target_pairs={{0,15},{1,0},{2,1},{3,2},{4,3},{5,4},{6,5},{7,6},{8,7},{9,8},{10,9... | collective-permute-start | bytes 786440 | tf_op jit(solution)/shard_map/ppermute | solution.py:29
  125.1 10.1 %collective-permute-start.4 = (bf16[8,64,256]{2,1,0:T(8,128)(2,1)S(1)}, bf16[8,64,256]{2,1,0:T(8,128)(2,1)S(1)}, u32[]{:S(2)}, u32[]{:S(2)}) collective-permute-start(bf16[8,64,256]{2,1,0:T(8,128)(2,1)S(1)} %collective-permute-done.3), channel_id=1, source_target_pairs={{0,1},{1,2},{2,3},{3,4},{4,5},{5,6},{6,7},{7,8},{8,9},{9,10},{10,1... | collective-permute-start | bytes 786440 | tf_op jit(solution)/shard_map/ppermute | solution.py:26
  125.1 15.8 %collective-permute-start.13 = (bf16[8,64,256]{2,1,0:T(8,128)(2,1)S(1)}, bf16[8,64,256]{2,1,0:T(8,128)(2,1)S(1)}, u32[]{:S(2)}, u32[]{:S(2)}) collective-permute-start(bf16[8,64,256]{2,1,0:T(8,128)(2,1)S(1)} %collective-permute-done.12), channel_id=1, source_target_pairs={{0,15},{1,0},{2,1},{3,2},{4,3},{5,4},{6,5},{7,6},{8,7},{9,8},{10,9... | collective-permute-start | bytes 786440 | tf_op jit(solution)/shard_map/ppermute | solution.py:29
  140.9 10.1 %collective-permute-start.5 = (bf16[8,64,256]{2,1,0:T(8,128)(2,1)S(1)}, bf16[8,64,256]{2,1,0:T(8,128)(2,1)S(1)}, u32[]{:S(2)}, u32[]{:S(2)}) collective-permute-start(bf16[8,64,256]{2,1,0:T(8,128)(2,1)S(1)} %collective-permute-done.4), channel_id=1, source_target_pairs={{0,1},{1,2},{2,3},{3,4},{4,5},{5,6},{6,7},{7,8},{8,9},{9,10},{10,1... | collective-permute-start | bytes 786440 | tf_op jit(solution)/shard_map/ppermute | solution.py:26
  140.9 24.3 %collective-permute-start.14 = (bf16[8,64,256]{2,1,0:T(8,128)(2,1)S(1)}, bf16[8,64,256]{2,1,0:T(8,128)(2,1)S(1)}, u32[]{:S(2)}, u32[]{:S(2)}) collective-permute-start(bf16[8,64,256]{2,1,0:T(8,128)(2,1)S(1)} %collective-permute-done.13), channel_id=1, source_target_pairs={{0,15},{1,0},{2,1},{3,2},{4,3},{5,4},{6,5},{7,6},{8,7},{9,8},{10,9... | collective-permute-start | bytes 786440 | tf_op jit(solution)/shard_map/ppermute | solution.py:29
  151.0 8.5 %collective-permute-start.6 = (bf16[8,64,256]{2,1,0:T(8,128)(2,1)S(1)}, bf16[8,64,256]{2,1,0:T(8,128)(2,1)S(1)}, u32[]{:S(2)}, u32[]{:S(2)}) collective-permute-start(bf16[8,64,256]{2,1,0:T(8,128)(2,1)S(1)} %collective-permute-done.5), channel_id=1, source_target_pairs={{0,1},{1,2},{2,3},{3,4},{4,5},{5,6},{6,7},{7,8},{8,9},{9,10},{10,1... | collective-permute-start | bytes 786440 | tf_op jit(solution)/shard_map/ppermute | solution.py:26
  165.2 8.5 %collective-permute-start.7 = (bf16[8,64,256]{2,1,0:T(8,128)(2,1)S(1)}, bf16[8,64,256]{2,1,0:T(8,128)(2,1)S(1)}, u32[]{:S(2)}, u32[]{:S(2)}) collective-permute-start(bf16[8,64,256]{2,1,0:T(8,128)(2,1)S(1)} %collective-permute-done.6), channel_id=1, source_target_pairs={{0,1},{1,2},{2,3},{3,4},{4,5},{5,6},{6,7},{7,8},{8,9},{9,10},{10,1... | collective-permute-start | bytes 786440 | tf_op jit(solution)/shard_map/ppermute | solution.py:26
  170.9 8.4 %copy-start.2 = (bf16[64,64,64]{2,1,0:T(8,128)(2,1)S(1)}, bf16[64,64,64]{2,1,0:T(8,128)(2,1)}, u32[]{:S(2)}) copy-start(bf16[64,64,64]{2,1,0:T(8,128)(2,1)} %convolution_bitcast_fusion.7) | copy-start | bytes 1572868
  170.9 8.4 %copy-start.3 = (bf16[64,64,64]{2,1,0:T(8,128)(2,1)S(1)}, bf16[64,64,64]{2,1,0:T(8,128)(2,1)}, u32[]{:S(2)}) copy-start(bf16[64,64,64]{2,1,0:T(8,128)(2,1)} %convolution_bitcast_fusion.6) | copy-start | bytes 1572868
  170.9 8.4 %copy-start.4 = (bf16[64,64,64]{2,1,0:T(8,128)(2,1)S(1)}, bf16[64,64,64]{2,1,0:T(8,128)(2,1)}, u32[]{:S(2)}) copy-start(bf16[64,64,64]{2,1,0:T(8,128)(2,1)} %convolution_bitcast_fusion.8) | copy-start | bytes 1572868
